TPU v7x, 128 devices: a whole 4x4x4 slice. The times are simulated.
128 devices in a mesh: req: 16 (over z, x), tp: 8 (over y, core).
Axes of the slice: x: 4, y: 4, z: 4, core: 2. Of those that a mesh axis runs over, the one named last changes fastest.
Arguments:
- tokens: bfloat16 [8192, 3072], P('req', 'tp'), may hold values from -3 to 3
- norm_gain: bfloat16 [3072], P('tp'), may hold values from 0.099609375 to 1.8984375
- w_query: bfloat16 [3072, 3072], P(None, 'tp'), may hold values from -0.3125 to 0.3125
- w_key: bfloat16 [3072, 3072], P(None, 'tp'), may hold values from -0.109375 to 0.109375
- w_value: bfloat16 [3072, 3072], P(None, 'tp'), may hold values from -0.109375 to 0.109375
- w_out: bfloat16 [3072, 3072], P('tp'), may hold values from -0.109375 to 0.109375
- prev_keys: bfloat16 [65536, 3072], P('req', 'tp'), may hold values from -300 to 300
- prev_values: bfloat16 [65536, 3072], P('req', 'tp'), may hold values from -6 to 6
- earlier_lengths: int32 [16, 4], P('req'), may hold values from 1 to 2048, 4096 in all within a row
- new_lengths: int32 [16, 4], P('req'), may hold values from 1 to 256, 512 in all within a row
- page_table: int32 [16, 36], P('req'), may hold values from 0 to 575, as said below
Outputs:
- layer_out: bfloat16 [8192, 3072], P('req', 'tp')
- decode_pool: bfloat16 [288, 8, 128, 1536], P('req', 'tp')
Inputs may be any that keep to these rules, and one draw needn't show every extreme that they name: `page_table`: every value appears exactly once. Among the pages of one index of req, at most 2 share the same value // 18, and in every draw some destination receives exactly 2 of them.
All inputs are finite; a program needn't handle non-finite values.
Results may differ from a plain program's by a relative error of at most 0.0075.
Values may be sent and summed in bfloat16 or wider, within the bound.
No kernel may reach another device: no remote copies, remote signals or barrier semaphores. Data moves between devices by JAX's collectives and lax.ppermute only.
A program may use at most 256 MiB of HBM per device.

v0:
```python
import math
import jax
import jax.numpy as jnp
from jax import lax
from jax.sharding import PartitionSpec as P

HD = 96
HG = 4
PAGE = 128
EPSILON = 1e-05
THETA = 10000.0


def from_partner(value, axis, distance):
    mask = 2**distance
    pairs = [(source, source ^ mask) for source in range(lax.axis_size(axis))]
    return lax.ppermute(value, axis, pairs)


def rotate(values, positions, head_size):
    count = values.shape[0]
    half_size = head_size // 2
    shaped = values.reshape(count, -1, head_size)
    freqs = jnp.exp(-math.log(THETA) * 2.0 * jnp.arange(half_size, dtype=jnp.float32) / head_size)
    angles = positions.astype(jnp.float32)[:, None] * freqs[None, :]
    cosine = jnp.cos(angles)[:, None, :]
    sine = jnp.sin(angles)[:, None, :]
    first = shaped[:, :, :half_size]
    second = shaped[:, :, half_size:]
    turned = jnp.concatenate(
        [first * cosine - second * sine, second * cosine + first * sine], axis=2
    )
    return turned.reshape(count, -1)


def request_ids(lengths, count):
    ends = jnp.cumsum(lengths)
    row_index = jnp.arange(count, dtype=jnp.int32)
    return jnp.sum((row_index[:, None] >= ends[None, :]).astype(jnp.int32), axis=1)


def block_layout(earlier, fresh, count):
    owners = request_ids(fresh, count)
    starts = jnp.cumsum(fresh) - fresh
    onehot = (owners[:, None] == jnp.arange(fresh.shape[0], dtype=jnp.int32)[None, :]).astype(
        jnp.int32
    )
    first_row = jnp.sum(onehot * starts[None, :], axis=1)
    before = jnp.sum(onehot * earlier[None, :], axis=1)
    row_index = jnp.arange(count, dtype=jnp.int32)
    return (owners, before + row_index - first_row)


def visible(earlier, owners, prev_count, count):
    prev_owner = request_ids(earlier, prev_count)
    row_index = jnp.arange(count, dtype=jnp.int32)
    old_part = owners[:, None] == prev_owner[None, :]
    new_part = (owners[:, None] == owners[None, :]) & (row_index[None, :] <= row_index[:, None])
    return jnp.concatenate([old_part, new_part], axis=1)


def order_pair(mine, partner, own_half):
    lower = jnp.where(own_half == 0, mine, partner)
    upper = jnp.where(own_half == 0, partner, mine)
    return jnp.stack([lower, upper], axis=1)


def join_heads(stacked, local_width):
    count, halves, rows_page = (stacked.shape[0], stacked.shape[1], stacked.shape[2])
    split_rows = stacked.reshape(count, halves, rows_page, 2, local_width)
    return split_rows.transpose(0, 2, 3, 1, 4).reshape(count, rows_page, 2 * halves * local_width)


def fill_pool(page_rows, slot_ids, slot_count):
    empty = jnp.zeros((slot_count + 1, page_rows.shape[1], page_rows.shape[2]), jnp.bfloat16)
    return empty.at[slot_ids].set(page_rows)[:slot_count][:, None]


def shards(
    tokens,
    norm_gain,
    w_query,
    w_key,
    w_value,
    w_out,
    prev_keys,
    prev_values,
    earlier_lengths,
    new_lengths,
    page_table,
):
    token_count, local_width = tokens.shape
    full_width = w_query.shape[0]
    widened = tokens.astype(jnp.float32)
    square_sums = lax.psum(jnp.sum(widened * widened, axis=1), "tp")
    scaling = lax.rsqrt(square_sums / full_width + EPSILON)
    normed = (widened * scaling[:, None] * norm_gain.astype(jnp.float32)[None, :]).astype(
        jnp.bfloat16
    )
    fragment = lax.all_gather(normed, "tp", axis=1, tiled=True)
    query_raw, key_raw, value_raw = tuple(
        (
            jnp.dot(fragment, weight, preferred_element_type=jnp.float32)
            for weight in (w_query, w_key, w_value)
        )
    )
    earlier = earlier_lengths[0]
    fresh = new_lengths[0]
    owners, positions = block_layout(earlier, fresh, token_count)
    queries = rotate(query_raw, positions, HD).astype(jnp.bfloat16)
    new_keys = rotate(key_raw, positions, HD).astype(jnp.bfloat16)
    new_values = value_raw.astype(jnp.bfloat16)
    keys_all = jnp.concatenate([prev_keys, new_keys], axis=0)
    values_all = jnp.concatenate([prev_values, new_values], axis=0)
    allowed = visible(earlier, owners, prev_keys.shape[0], token_count)
    heads_here = local_width // HD
    scores = jnp.einsum(
        "qhd,khd->hqk",
        queries.reshape(token_count, heads_here, HD),
        keys_all.reshape(-1, heads_here, HD),
        preferred_element_type=jnp.float32,
    ) * HD ** (-0.5)
    scores = jnp.where(allowed[None, :, :], scores, -1e30)
    row_peak = jnp.max(scores, axis=2, keepdims=True)
    weights = jnp.exp(scores - row_peak)
    totals = jnp.sum(weights, axis=2)
    prob_rows = weights.astype(jnp.bfloat16)
    mixture = jnp.einsum(
        "hqk,khd->qhd",
        prob_rows,
        values_all.reshape(-1, heads_here, HD),
        preferred_element_type=jnp.float32,
    )
    attended = (
        (mixture / totals.T[:, :, None]).astype(jnp.bfloat16).reshape(token_count, local_width)
    )
    projected = jnp.dot(attended, w_out, preferred_element_type=jnp.float32)
    summed = lax.psum_scatter(projected, "tp", scatter_dimension=1, tiled=True)
    layer_out = (tokens.astype(jnp.float32) + summed).astype(jnp.bfloat16)
    page_total = keys_all.shape[0] // PAGE
    page_rows = jnp.concatenate(
        [
            keys_all.reshape(page_total, PAGE, local_width),
            values_all.reshape(page_total, PAGE, local_width),
        ],
        axis=2,
    )
    req_count = lax.axis_size("req")
    halves = lax.axis_size("tp") // HG
    slot_count = page_total // halves
    dest_count = req_count * halves
    capacity = 2 * ((page_total // 2 + dest_count - 1) // dest_count)
    table = page_table[0]
    target = table // slot_count
    slot_ids = table % slot_count
    own_half = lax.axis_index("tp") % halves
    order_index = jnp.arange(page_total, dtype=jnp.int32)
    earlier_mask = order_index[:, None] > order_index[None, :]
    placing = jnp.sum(
        ((target[:, None] == target[None, :]) & earlier_mask).astype(jnp.int32), axis=1
    )
    bucket = target * capacity + placing
    send_rows = (
        jnp.zeros((dest_count * capacity, PAGE, 2 * local_width), jnp.bfloat16)
        .at[bucket]
        .set(page_rows)
    )
    send_slots = jnp.full((dest_count * capacity,), slot_count, jnp.int32).at[bucket].set(slot_ids)
    got_rows, got_slots = (
        lax.all_to_all(send_rows, "req", split_axis=0, concat_axis=0, tiled=True),
        lax.all_to_all(send_slots, "req", split_axis=0, concat_axis=0, tiled=True),
    )
    got_rows = got_rows.reshape(req_count, halves, capacity, PAGE, 2 * local_width)
    got_slots = got_slots.reshape(req_count, halves, capacity)
    mine = lax.dynamic_index_in_dim(got_rows, own_half, 1, keepdims=False).reshape(
        req_count * capacity, PAGE, 2 * local_width
    )
    final_slots = lax.dynamic_index_in_dim(got_slots, own_half, 1, keepdims=False).reshape(-1)
    other = lax.dynamic_index_in_dim(got_rows, 1 - own_half, 1, keepdims=False).reshape(
        req_count * capacity, PAGE, 2 * local_width
    )
    partner = from_partner(other, "tp", 0)
    stacked = order_pair(mine, partner, own_half)
    final_rows = join_heads(stacked, local_width)
    decode_pool = fill_pool(final_rows, final_slots, slot_count)
    return (layer_out, decode_pool)


def solution(mesh):
    placed = (
        P("req", "tp"),
        P("tp"),
        P(None, "tp"),
        P(None, "tp"),
        P(None, "tp"),
        P("tp", None),
        P("req", "tp"),
        P("req", "tp"),
        P("req", None),
        P("req", None),
        P("req", None),
    )
    return jax.shard_map(
        shards,
        mesh=mesh,
        in_specs=placed,
        out_specs=(P("req", "tp"), P("req", "tp", None, None)),
        check_vma=False,
    )
```

profile of v0, /device:TPU:1, one launch (start us, length us, event | category | flops | bytes accessed | tf_op | source)
XLA Modules:
  0.0 441.5 jit_solution(15881802135246873474)
XLA Ops:
  9.2 13.5 %psum.7 = f32[512]{0:T(512)S(1)} all-reduce(f32[512]{0:T(512)S(1)} %fusion.16), channel_id=1, replica_groups=mesh['req'=16,'tp'=8] {'tp'}, use_global_device_ids=true, to_apply=%region_1.0 | all-reduce | flops 512 | bytes 4096 | tf_op jit(solution)/shard_map/psum | solution.py:95
  22.7 1.9 fusion.18
  32.0 1.6 pad_add_fusion
  33.6 21.3 %all-gather.2.cloned.1.call-done = bf16[512,3072]{1,0:T(8,128)(2,1)} async-done(((bf16[512,384]{1,0:T(8,128)(2,1)}), bf16[512,3072]{1,0:T(8,128)(2,1)}) %all-gather.2.cloned.1.call-update) | async-done | bytes 3145744 | tf_op jit(solution)/shard_map/all_gather | solution.py:100
  54.9 4.2 fusion.38
  59.2 1.4 fusion.37
  61.1 4.0 pad_maximum_fusion.2
  65.1 5.8 %copy.54 = bf16[4608,384]{0,1:T(8,128)(2,1)} copy(bf16[4608,384]{1,0:T(8,128)(2,1)} %pad_maximum_fusion.2) | data formatting | bytes 7077888 | tf_op jit(solution)/shard_map/concatenate | solution.py:113
  70.9 4.5 %convolution_convert_fusion = bf16[512,384]{1,0:T(8,128)(2,1)S(1)} fusion(bf16[512,3072]{1,0:T(8,128)(2,1)} %all-gather.2.cloned.1.call-done, bf16[3072,384]{1,0:T(8,128)(2,1)} %param.15), kind=kOutput, calls=%fused_computation.20 | convolution fusion | flops 1208156160 | bytes 5898240 | tf_op jit(solution)/shard_map/dot_general | solution.py:103
  75.8 7.1 %pad_maximum_fusion = bf16[36,128,768]{2,1,0:T(8,128)(2,1)} fusion(bf16[36,128,384]{2,1,0:T(8,128)(2,1)S(1)} %bitcast.89, bf16[36,128,384]{2,1,0:T(8,128)(2,1)} %bitcast.90), kind=kLoop, calls=%fused_computation.13 | loop fusion | flops 14155776 | bytes 14155776 | tf_op jit(solution)/shard_map/concatenate | solution.py:141
  82.9 6.0 %broadcast_in_dim.20 = bf16[64,128,768]{2,1,0:T(8,128)(2,1)} broadcast(bf16[]{:T(256)} %constant.76.clone.1), dimensions={} | broadcast | bytes 12582914 | tf_op jit(solution)/shard_map/broadcast_in_dim | solution.py:164
  88.9 22.5 %scatter_fusion = bf16[64,128,768]{2,1,0:T(8,128)(2,1)} fusion(bf16[64,128,768]{2,1,0:T(8,128)(2,1)} %broadcast_in_dim.20, s32[36]{0:T(128)S(1)} %fusion.29, bf16[36,128,768]{2,1,0:T(8,128)(2,1)} %pad_maximum_fusion), kind=kCustom, calls=%fused_computation.1 | custom fusion | bytes 21233808 | tf_op jit(solution)/shard_map/scatter | solution.py:166
  111.4 6.7 %all-to-all-start.1 = ((bf16[64,128,768]{2,1,0:T(8,128)(2,1)}), bf16[64,128,768]{2,1,0:T(8,128)(2,1)}, u32[]{:S(2)}, u32[]{:S(2)}) async-start(bf16[64,128,768]{2,1,0:T(8,128)(2,1)} %scatter_fusion), calls=%async_computation.2 | async-start | bytes 25165824 | tf_op jit(solution)/shard_map/all_to_all | solution.py:170
  118.3 18.6 %fusion = (f32[4,512]{1,0:T(4,128)S(1)}, f32[4,512,4608]{2,1,0:T(8,128)}) fusion(pred[512,4608]{1,0:T(8,128)(4,1)} %pad_add_fusion, bf16[4608,4,96]{0,2,1:T(8,128)(2,1)} %bitcast.94, bf16[512,4,48]{0,2,1:T(8,128)(2,1)S(1)} %get-tuple-element.17, bf16[512,4,48]{0,2,1:T(8,128)(2,1)S(1)} %get-tuple-element.16), kind=kOutput, calls=%fused_computation.5 | convolution fusion | flops 1841035264 | bytes 44048384 | tf_op jit(solution)/shard_map/qhd,khd->hqk/dot_general | solution.py:117
  136.8 5.7 %copy.52 = bf16[4608,384]{0,1:T(8,128)(2,1)} copy(bf16[4608,384]{1,0:T(8,128)(2,1)} %copy-done.1) | data formatting | bytes 7077888 | tf_op jit(solution)/shard_map/concatenate | solution.py:114
  142.6 18.2 %fusion.1 = f32[4,512]{1,0:T(4,128)S(1)} fusion(f32[4,512,4608]{2,1,0:T(8,128)} %get-tuple-element.26, f32[4,512]{1,0:T(4,128)S(1)} %get-tuple-element.25, pred[512,4608]{1,0:T(8,128)(4,1)} %pad_add_fusion), kind=kLoop, calls=%fused_computation.6 | loop fusion | flops 37746688 | bytes 40124416 | tf_op jit(solution)/shard_map/reduce_sum | solution.py:126
  160.8 15.3 %fusion.12 = bf16[512,4,96]{0,2,1:T(8,128)(2,1)S(1)} fusion(bf16[4608,4,96]{0,2,1:T(8,128)(2,1)S(1)} %bitcast.95, f32[4,512,4608]{2,1,0:T(8,128)} %get-tuple-element.26, f32[4,512]{1,0:T(4,128)S(1)} %get-tuple-element.25, pred[512,4608]{1,0:T(8,128)(4,1)S(1)} %copy-done.2, f32[512,4]{0,1:T(4,128)S(1)} %bitcast.100), kind=kOutput, calls=%fused_computation.25 | convolution fusion | flops 1850081280 | bytes 44056576 | tf_op jit(solution)/shard_map/hqk,khd->qhd/dot_general | solution.py:128
  176.2 4.5 %fusion.39 = f32[512,3072]{1,0:T(8,128)} fusion(bf16[512,384]{0,1:T(8,128)(2,1)S(1)} %bitcast.99, bf16[384,3072]{1,0:T(8,128)(2,1)S(1)} %copy-done), kind=kOutput, calls=%fused_computation.83 | convolution fusion | flops 1207959552 | bytes 9043968 | tf_op jit(solution)/shard_map/dot_general | solution.py:137
  180.7 125.3 %all-to-all-done.1 = bf16[64,128,768]{2,1,0:T(8,128)(2,1)} async-done(((bf16[64,128,768]{2,1,0:T(8,128)(2,1)}), bf16[64,128,768]{2,1,0:T(8,128)(2,1)}, u32[]{:S(2)}, u32[]{:S(2)}) %all-to-all-start.1) | async-done | bytes 12582944 | tf_op jit(solution)/shard_map/all_to_all | solution.py:170
  306.0 10.7 %constant_dynamic-slice_fusion = (bf16[16,1,2,128,768]{4,3,2,1,0:T(8,128)(2,1)}, bf16[16,1,2,128,768]{4,3,2,1,0:T(8,128)(2,1)}) fusion(bf16[16,2,2,128,768]{4,3,2,1,0:T(8,128)(2,1)} %bitcast.28, s32[]{:T(128)S(6)} %select_n.86, s32[]{:T(128)S(6)} %select_n.89), kind=kLoop, calls=%fused_computation.63 | loop fusion | bytes 25165832 | tf_op jit(solution)/shard_map/jit(dynamic_index_in_dim)/dynamic_slice | solution.py:175
  319.5 3.7 all-to-all-start
  323.2 6.0 %all-to-all-done = s32[16,4,1]{1,2,0:T(1,128)S(1)} async-done(((s32[16,4,1]{1,2,0:T(1,128)}), s32[16,4,1]{1,2,0:T(1,128)S(1)}, u32[]{:S(2)}, u32[]{:S(2)}) %all-to-all-start) | async-done | bytes 288 | tf_op jit(solution)/shard_map/all_to_all | solution.py:171
  329.5 2.0 fusion.19
  331.5 10.3 %bitcast_select_fusion.1 = (bf16[32,128,768]{2,1,0:T(8,128)(2,1)}, bf16[32,128,768]{2,1,0:T(8,128)(2,1)}) fusion(bf16[32,128,768]{2,1,0:T(8,128)(2,1)} %collective-permute-done, bf16[16,1,2,128,768]{4,3,2,1,0:T(8,128)(2,1)} %get-tuple-element.14, pred[]{:T(512)S(6)} %eq.75), kind=kLoop, calls=%fused_computation.15 | loop fusion | flops 6291456 | bytes 25165824 | tf_op jit(solution)/shard_map/jit(_where)/select_n | solution.py:63
  341.8 8.7 %copy.58 = bf16[32,128,768]{1,2,0:T(8,128)(2,1)} copy(bf16[32,128,768]{2,1,0:T(8,128)(2,1)} %get-tuple-element.12) | data formatting | bytes 12582912 | tf_op jit(solution)/shard_map/jit(_where)/select_n | solution.py:63
  350.5 8.6 %copy.59 = bf16[32,128,768]{1,2,0:T(8,128)(2,1)} copy(bf16[32,128,768]{2,1,0:T(8,128)(2,1)} %get-tuple-element.13) | data formatting | bytes 12582912 | tf_op jit(solution)/shard_map/jit(_where)/select_n | solution.py:64
  359.1 6.2 %maximum_bitcast_fusion = bf16[32,128,2,2,384]{1,4,2,0,3:T(8,128)(2,1)S(1)} fusion(bf16[32,1,128,2,384]{2,4,3,0,1:T(8,128)(2,1)} %bitcast.92, bf16[32,1,128,2,384]{2,4,3,0,1:T(8,128)(2,1)} %bitcast.91), kind=kLoop, calls=%fused_computation.10 | loop fusion | flops 6291456 | bytes 25165824 | tf_op jit(solution)/shard_map/transpose | solution.py:71
  365.3 5.7 %copy.60 = bf16[32,128,2,2,384]{1,4,3,2,0:T(8,128)(2,1)} copy(bf16[32,128,2,2,384]{1,4,2,0,3:T(8,128)(2,1)S(1)} %maximum_bitcast_fusion) | data formatting | bytes 25165824 | tf_op jit(solution)/shard_map/transpose | solution.py:71
  371.0 16.6 %copy.61 = bf16[32,128,1536]{2,1,0:T(8,128)(2,1)} copy(bf16[32,128,1536]{1,2,0:T(8,128)(2,1)} %bitcast.88) | data formatting | bytes 25165824 | tf_op jit(solution)/shard_map/reshape | solution.py:71
  387.6 3.7 broadcast_in_dim.18
  391.4 36.8 %scatter_fusion.1 = bf16[19,128,1536]{2,1,0:T(8,128)(2,1)} fusion(bf16[19,128,1536]{2,1,0:T(8,128)(2,1)} %broadcast_in_dim.18, s32[32]{0:T(128)S(1)} %fusion.30, bf16[32,128,1536]{2,1,0:T(8,128)(2,1)} %copy.61), kind=kCustom, calls=%fused_computation.2 | custom fusion | bytes 37748864 | tf_op jit(solution)/shard_map/scatter | solution.py:76
  428.1 6.6 %slice_bitcast_fusion = bf16[18,1,128,1536]{3,2,1,0:T(8,128)(2,1)} fusion(bf16[19,128,1536]{2,1,0:T(8,128)(2,1)} %scatter_fusion.1), kind=kLoop, calls=%fused_computation.12 | loop fusion | bytes 14155776
  (52 shorter events, 13.6 us)
Async XLA Ops:
  7.2 169.0 %copy-start = (bf16[384,3072]{1,0:T(8,128)(2,1)S(1)}, bf16[384,3072]{1,0:T(8,128)(2,1)}, u32[]{:S(2)}) copy-start(bf16[384,3072]{1,0:T(8,128)(2,1)} %param.16) | copy-start | bytes 7077892
  7.2 47.7 %all-gather.2.cloned.1.call-start = ((), (), s32[]{:S(2)}) async-start(), calls=%async_computation.3 | async-start | bytes 3538944 | tf_op jit(solution)/shard_map/all_gather | solution.py:100
  54.9 4.2 copy-start.6
  54.9 4.3 copy-start.7
  70.9 4.6 %copy-start.5 = (bf16[4096,384]{1,0:T(8,128)(2,1)S(1)}, bf16[4096,384]{1,0:T(8,128)(2,1)}, u32[]{:S(2)}) copy-start(bf16[4096,384]{1,0:T(8,128)(2,1)} %param.18) | copy-start | bytes 9437188
  75.8 7.1 %copy-start.1 = (bf16[4608,384]{1,0:T(8,128)(2,1)}, bf16[4608,384]{1,0:T(8,128)(2,1)S(1)}, u32[]{:S(2)}) copy-start(bf16[4608,384]{1,0:T(8,128)(2,1)S(1)} %pad_maximum_fusion.1) | copy-start | bytes 10616836
  111.4 194.7 %all-to-all-start.1 = ((bf16[64,128,768]{2,1,0:T(8,128)(2,1)}), bf16[64,128,768]{2,1,0:T(8,128)(2,1)}, u32[]{:S(2)}, u32[]{:S(2)}) async-start(bf16[64,128,768]{2,1,0:T(8,128)(2,1)} %scatter_fusion), calls=%async_computation.2 | async-start | bytes 25165824 | tf_op jit(solution)/shard_map/all_to_all | solution.py:170
  118.0 211.5 %reduce-scatter.2.cloned.1.call-start = ((), (), s32[]{:S(2)}) async-start(), calls=%async_computation.4 | async-start | bytes 7077888 | tf_op jit(solution)/shard_map/reduce_scatter | solution.py:138
  142.6 18.2 %copy-start.2 = (pred[512,4608]{1,0:T(8,128)(4,1)S(1)}, pred[512,4608]{1,0:T(8,128)(4,1)}, u32[]{:S(2)}) copy-start(pred[512,4608]{1,0:T(8,128)(4,1)} %pad_add_fusion) | copy-start | bytes 7077892
  142.6 18.2 %copy-start.3 = (bf16[4608,384]{0,1:T(8,128)(2,1)S(1)}, bf16[4608,384]{0,1:T(8,128)(2,1)}, u32[]{:S(2)}) copy-start(bf16[4608,384]{0,1:T(8,128)(2,1)} %copy.52) | copy-start | bytes 10616836
  306.0 23.5 %copy-start.4 = (bf16[512,384]{1,0:T(8,128)(2,1)S(1)}, bf16[512,384]{1,0:T(8,128)(2,1)}, u32[]{:S(2)}) copy-start(bf16[512,384]{1,0:T(8,128)(2,1)} %param.11) | copy-start | bytes 1179652
  316.7 14.8 %collective-permute-start = (bf16[32,128,768]{2,1,0:T(8,128)(2,1)}, bf16[32,128,768]{2,1,0:T(8,128)(2,1)}, u32[]{:S(2)}, u32[]{:S(2)}) collective-permute-start(bf16[32,128,768]{2,1,0:T(8,128)(2,1)} %bitcast.93), channel_id=1, source_target_pairs={{0,1},{1,0},{2,3},{3,2},{4,5},{5,4},{6,7},{7,6},{8,9},{9,8},{10,11... | collective-permute-start | bytes 18874376 | tf_op jit(solution)/shard_map/ppermute | solution.py:17
  319.5 9.7 %all-to-all-start = ((s32[16,4,1]{1,2,0:T(1,128)}), s32[16,4,1]{1,2,0:T(1,128)S(1)}, u32[]{:S(2)}, u32[]{:S(2)}) async-start(s32[16,4,1]{1,2,0:T(1,128)} %bitcast.23), calls=%async_computation.1 | async-start | bytes 16384 | tf_op jit(solution)/shard_map/all_to_all | solution.py:171
Sparse Core Ops, SparseCore 0:
  24.7 30.1 all-gather.1
  180.8 41.9 reduce-scatter.1
where the time goes:
time: 444 us; the launch traced here: 442 us
  waiting for transfers between devices  153 us (34%)
  local copies, waits for them, and re-layouts  139 us (31%)
  other arithmetic  61.3 us (14%)
  matrix products  48.6 us (11%)
  between operations  14.3 us (3%)
  blocking collectives  13.5 us (3%)
  starting transfers between devices  12 us (3%)
    all_to_all x1, waiting for transfers between devices, shards(): lax.all_to_all(send_rows, 'req', split_axis=0, concat_axis=0, tiled=True)  125 us
    scatter x1, local copies, waits for them, and re-layouts, fill_pool(): return empty.at[slot_ids].set(page_rows)[:slot_count][:, None]  36.8 us
    scatter x1, local copies, waits for them, and re-layouts, shards(): send_rows = jnp.zeros((dest_count * capacity, PAGE, 2 * local_width), jnp...  22.5 us
    all_gather x1, waiting for transfers between devices, shards(): fragment = lax.all_gather(normed, 'tp', axis=1, tiled=True)  21.3 us
    dot_general x1, matrix products, shards(): jnp.einsum('qhd,khd->hqk', queries.reshape(token_count, heads_here, HD),...  18.6 us
    reduce_sum x1, other arithmetic, shards(): totals = jnp.sum(weights, axis=2)  18.2 us
    reshape x1, local copies, waits for them, and re-layouts, join_heads(): split_rows.transpose(0, 2, 3, 1, 4)  16.6 us
    dot_general x1, matrix products, shards(): jnp.einsum('hqk,khd->qhd', prob_rows, values_all.reshape(-1, heads_here,...  15.3 us
  transfers between devices with their start and end apart: 5, of which 3 were waited for; matrix products, arithmetic and copies ran while one was open for 19% of the time, Pallas kernels for 0%

commit v1 on v0

--- a/solution.py
+++ b/solution.py
@@ -97,7 +97,16 @@
     normed = (widened * scaling[:, None] * norm_gain.astype(jnp.float32)[None, :]).astype(
         jnp.bfloat16
     )
-    fragment = lax.all_gather(normed, "tp", axis=1, tiled=True)
+    ways = lax.axis_size("tp")
+    up = [(d, (d + 1) % ways) for d in range(ways)]
+    down = [(d, (d - 1) % ways) for d in range(ways)]
+    earlier_2, later = ([normed], [normed])
+    for _ in range(ways // 2):
+        earlier_2.append(lax.ppermute(earlier_2[-1], "tp", up))
+    for _ in range((ways - 1) // 2):
+        later.append(lax.ppermute(later[-1], "tp", down))
+    line = jnp.concatenate([*earlier_2[::-1], *later[1:]], axis=1)
+    fragment = jnp.roll(line, (lax.axis_index("tp") - ways // 2) * normed.shape[1], axis=1)
     query_raw, key_raw, value_raw = tuple(
         (
             jnp.dot(fragment, weight, preferred_element_type=jnp.float32)

time: 444 us -> 450 us (1.014)
  waiting for transfers between devices: 153 us -> 122 us
  starting transfers between devices: 12 us -> 39.6 us
  local copies, waits for them, and re-layouts: 139 us -> 150 us
    all_gather x1 -> x0, waiting for transfers between devices: 21.3 us -> none  [shards(): fragment = lax.all_gather(normed, 'tp', axis=1, tiled=True)]
    all_to_all x1, waiting for transfers between devices: 125 us -> 108 us  [shards(): lax.all_to_all(send_rows, 'req', split_axis=0, concat_axis=0, tiled=True)]
    ppermute x0 -> x7, starting transfers between devices: none -> 16.8 us  [the longest x3 9.32 us: shards(): later.append(lax.ppermute(later[-1], 'tp', down))]
    unnamed x17 -> x46, local copies, waits for them, and re-layouts: 6.66 us -> 16.9 us
    ppermute x0 -> x7, waiting for transfers between devices: none -> 7.75 us  [the longest x4 7.64 us: shards(): earlier_2.append(lax.ppermute(earlier_2[-1], 'tp', up))]
    ppermute x1, starting transfers between devices: 1.36 us -> 8.51 us  [from_partner(): return lax.ppermute(value, axis, pairs)]
  transfers between devices with their start and end apart: 5 -> 11, of which waited for: 3 -> 7; matrix products, arithmetic and copies ran while one was open for 19% -> 20% of each run, Pallas kernels for 0% -> 0%
where the time goes in v1:
time: 450 us; the launch traced here: 446 us
  local copies, waits for them, and re-layouts  150 us (33%)
  waiting for transfers between devices  122 us (27%)
  other arithmetic  61.3 us (14%)
  matrix products  44.9 us (10%)
  starting transfers between devices  39.6 us (9%)
  between operations  14.5 us (3%)
  blocking collectives  13.5 us (3%)
    all_to_all x1, waiting for transfers between devices, shards(): lax.all_to_all(send_rows, 'req', split_axis=0, concat_axis=0, tiled=True)  108 us
    scatter x1, local copies, waits for them, and re-layouts, fill_pool(): return empty.at[slot_ids].set(page_rows)[:slot_count][:, None]  36.8 us
    scatter x1, local copies, waits for them, and re-layouts, shards(): send_rows = jnp.zeros((dest_count * capacity, PAGE, 2 * local_width), jnp...  22.5 us
    dot_general x1, matrix products, shards(): jnp.einsum('qhd,khd->hqk', queries.reshape(token_count, heads_here, HD),...  18.6 us
    reduce_sum x1, other arithmetic, shards(): totals = jnp.sum(weights, axis=2)  18.2 us
    unnamed x46, local copies, waits for them, and re-layouts  16.9 us
    reshape x1, local copies, waits for them, and re-layouts, join_heads(): split_rows.transpose(0, 2, 3, 1, 4)  16.6 us
    dot_general x1, matrix products, shards(): jnp.einsum('hqk,khd->qhd', prob_rows, values_all.reshape(-1, heads_here,...  15.3 us
  transfers between devices with their start and end apart: 11, of which 7 were waited for; matrix products, arithmetic and copies ran while one was open for 20% of the time, Pallas kernels for 0%

profile of v1, /device:TPU:1, one launch (start us, length us, event | category | flops | bytes accessed | tf_op | source)
XLA Modules:
  0.0 446.2 jit_solution(17304116291206696440)
XLA Ops:
  9.2 13.5 %psum.7 = f32[512]{0:T(512)S(1)} all-reduce(f32[512]{0:T(512)S(1)} %fusion.25), channel_id=1, replica_groups=mesh['req'=16,'tp'=8] {'tp'}, use_global_device_ids=true, to_apply=%region_1.0 | all-reduce | flops 512 | bytes 4096 | tf_op jit(solution)/shard_map/psum | solution.py:95
  24.6 2.9 collective-permute-start.4
  35.1 5.0 %collective-permute-done.1 = bf16[512,384]{1,0:T(8,128)(2,1)S(1)} collective-permute-done((bf16[512,384]{1,0:T(8,128)(2,1)}, bf16[512,384]{1,0:T(8,128)(2,1)S(1)}, u32[]{:S(2)}, u32[]{:S(2)}) %collective-permute-start.1) | collective-permute-done | bytes 393248 | tf_op jit(solution)/shard_map/ppermute | solution.py:105
  42.8 2.9 collective-permute-start.5
  47.2 2.6 collective-permute-start.3
  50.4 3.6 collective-permute-start.6
  65.8 2.6 fusion.15
  74.3 4.2 pad_maximum_fusion.2
  78.5 5.8 %copy.54 = bf16[4608,384]{0,1:T(8,128)(2,1)} copy(bf16[4608,384]{1,0:T(8,128)(2,1)} %pad_maximum_fusion.2) | data formatting | bytes 7077888 | tf_op jit(solution)/shard_map/concatenate | solution.py:122
  86.5 7.1 %pad_maximum_fusion = bf16[36,128,768]{2,1,0:T(8,128)(2,1)} fusion(bf16[36,128,384]{2,1,0:T(8,128)(2,1)S(1)} %bitcast.86, bf16[36,128,384]{2,1,0:T(8,128)(2,1)} %bitcast.87), kind=kLoop, calls=%fused_computation.13 | loop fusion | flops 14155776 | bytes 14155776 | tf_op jit(solution)/shard_map/concatenate | solution.py:150
  93.6 6.0 %broadcast_in_dim.20 = bf16[64,128,768]{2,1,0:T(8,128)(2,1)} broadcast(bf16[]{:T(256)} %constant.100.clone.1), dimensions={} | broadcast | bytes 12582914 | tf_op jit(solution)/shard_map/broadcast_in_dim | solution.py:173
  99.6 22.5 %scatter_fusion = bf16[64,128,768]{2,1,0:T(8,128)(2,1)} fusion(bf16[64,128,768]{2,1,0:T(8,128)(2,1)} %broadcast_in_dim.20, s32[36]{0:T(128)S(1)} %fusion.41, bf16[36,128,768]{2,1,0:T(8,128)(2,1)} %pad_maximum_fusion), kind=kCustom, calls=%fused_computation.1 | custom fusion | bytes 21233808 | tf_op jit(solution)/shard_map/scatter | solution.py:175
  122.1 7.8 %all-to-all-start.1 = ((bf16[64,128,768]{2,1,0:T(8,128)(2,1)}), bf16[64,128,768]{2,1,0:T(8,128)(2,1)}, u32[]{:S(2)}, u32[]{:S(2)}) async-start(bf16[64,128,768]{2,1,0:T(8,128)(2,1)} %scatter_fusion), calls=%async_computation.2 | async-start | bytes 25165824 | tf_op jit(solution)/shard_map/all_to_all | solution.py:179
  129.9 18.6 %fusion = (f32[4,512]{1,0:T(4,128)S(1)}, f32[4,512,4608]{2,1,0:T(8,128)}) fusion(pred[512,4608]{1,0:T(8,128)(4,1)} %pad_add_fusion, bf16[4608,4,96]{0,2,1:T(8,128)(2,1)} %bitcast.91, bf16[512,4,48]{0,2,1:T(8,128)(2,1)S(1)} %copy-done.9, bf16[512,4,48]{0,2,1:T(8,128)(2,1)S(1)} %copy-done.8), kind=kOutput, calls=%fused_computation.5 | convolution fusion | flops 1841035264 | bytes 44048384 | tf_op jit(solution)/shard_map/qhd,khd->hqk/dot_general | solution.py:126
  148.5 5.7 %copy.52 = bf16[4608,384]{0,1:T(8,128)(2,1)} copy(bf16[4608,384]{1,0:T(8,128)(2,1)} %copy-done.1) | data formatting | bytes 7077888 | tf_op jit(solution)/shard_map/concatenate | solution.py:123
  154.2 18.2 %fusion.1 = f32[4,512]{1,0:T(4,128)S(1)} fusion(f32[4,512,4608]{2,1,0:T(8,128)} %get-tuple-element.26, f32[4,512]{1,0:T(4,128)S(1)} %get-tuple-element.25, pred[512,4608]{1,0:T(8,128)(4,1)} %pad_add_fusion), kind=kLoop, calls=%fused_computation.6 | loop fusion | flops 37746688 | bytes 40124416 | tf_op jit(solution)/shard_map/reduce_sum | solution.py:135
  172.5 15.3 %fusion.21 = bf16[512,4,96]{0,2,1:T(8,128)(2,1)S(1)} fusion(bf16[4608,4,96]{0,2,1:T(8,128)(2,1)S(1)} %bitcast.92, f32[4,512,4608]{2,1,0:T(8,128)} %get-tuple-element.26, f32[4,512]{1,0:T(4,128)S(1)} %get-tuple-element.25, pred[512,4608]{1,0:T(8,128)(4,1)S(1)} %copy-done.3, f32[512,4]{0,1:T(4,128)S(1)} %bitcast.97), kind=kOutput, calls=%fused_computation.31 | convolution fusion | flops 1850081280 | bytes 44056576 | tf_op jit(solution)/shard_map/hqk,khd->qhd/dot_general | solution.py:137
  187.8 4.5 %fusion.49 = f32[512,3072]{1,0:T(8,128)} fusion(bf16[512,384]{0,1:T(8,128)(2,1)S(1)} %bitcast.96, bf16[384,3072]{1,0:T(8,128)(2,1)S(1)} %copy-done), kind=kOutput, calls=%fused_computation.106 | convolution fusion | flops 1207959552 | bytes 9043968 | tf_op jit(solution)/shard_map/dot_general | solution.py:146
  192.4 108.1 %all-to-all-done.1 = bf16[64,128,768]{2,1,0:T(8,128)(2,1)} async-done(((bf16[64,128,768]{2,1,0:T(8,128)(2,1)}), bf16[64,128,768]{2,1,0:T(8,128)(2,1)}, u32[]{:S(2)}, u32[]{:S(2)}) %all-to-all-start.1) | async-done | bytes 12582944 | tf_op jit(solution)/shard_map/all_to_all | solution.py:179
  300.5 10.7 %constant_dynamic-slice_fusion.1 = (bf16[16,1,2,128,768]{4,3,2,1,0:T(8,128)(2,1)}, bf16[16,1,2,128,768]{4,3,2,1,0:T(8,128)(2,1)}) fusion(bf16[16,2,2,128,768]{4,3,2,1,0:T(8,128)(2,1)} %bitcast.28, s32[]{:T(128)S(6)} %select_n.100, s32[]{:T(128)S(6)} %select_n.103), kind=kLoop, calls=%fused_computation.86 | loop fusion | bytes 25165832 | tf_op jit(solution)/shard_map/jit(dynamic_index_in_dim)/dynamic_slice | solution.py:184
  311.1 8.5 %collective-permute-start.7 = (bf16[32,128,768]{2,1,0:T(8,128)(2,1)}, bf16[32,128,768]{2,1,0:T(8,128)(2,1)}, u32[]{:S(2)}, u32[]{:S(2)}) collective-permute-start(bf16[32,128,768]{2,1,0:T(8,128)(2,1)} %bitcast.90), channel_id=1, source_target_pairs={{0,1},{1,0},{2,3},{3,2},{4,5},{5,4},{6,7},{7,6},{8,9},{9,8},{10,11... | collective-permute-start | bytes 18874376 | tf_op jit(solution)/shard_map/ppermute | solution.py:17
  321.0 6.5 %all-to-all-start = ((s32[16,4,1]{1,2,0:T(1,128)}), s32[16,4,1]{1,2,0:T(1,128)S(1)}, u32[]{:S(2)}, u32[]{:S(2)}) async-start(s32[16,4,1]{1,2,0:T(1,128)} %bitcast.23), calls=%async_computation.1 | async-start | bytes 16384 | tf_op jit(solution)/shard_map/all_to_all | solution.py:180
  327.6 6.3 %all-to-all-done = s32[16,4,1]{1,2,0:T(1,128)S(1)} async-done(((s32[16,4,1]{1,2,0:T(1,128)}), s32[16,4,1]{1,2,0:T(1,128)S(1)}, u32[]{:S(2)}, u32[]{:S(2)}) %all-to-all-start) | async-done | bytes 288 | tf_op jit(solution)/shard_map/all_to_all | solution.py:180
  336.1 10.3 %bitcast_select_fusion.1 = (bf16[32,128,768]{2,1,0:T(8,128)(2,1)}, bf16[32,128,768]{2,1,0:T(8,128)(2,1)}) fusion(bf16[32,128,768]{2,1,0:T(8,128)(2,1)} %collective-permute-done.7, bf16[16,1,2,128,768]{4,3,2,1,0:T(8,128)(2,1)} %get-tuple-element.14, pred[]{:T(512)S(6)} %eq.78), kind=kLoop, calls=%fused_computation.15 | loop fusion | flops 6291456 | bytes 25165824 | tf_op jit(solution)/shard_map/jit(_where)/select_n | solution.py:63
  346.5 8.7 %copy.58 = bf16[32,128,768]{1,2,0:T(8,128)(2,1)} copy(bf16[32,128,768]{2,1,0:T(8,128)(2,1)} %get-tuple-element.12) | data formatting | bytes 12582912 | tf_op jit(solution)/shard_map/jit(_where)/select_n | solution.py:63
  355.2 8.6 %copy.59 = bf16[32,128,768]{1,2,0:T(8,128)(2,1)} copy(bf16[32,128,768]{2,1,0:T(8,128)(2,1)} %get-tuple-element.13) | data formatting | bytes 12582912 | tf_op jit(solution)/shard_map/jit(_where)/select_n | solution.py:64
  363.8 6.2 %maximum_bitcast_fusion = bf16[32,128,2,2,384]{1,4,2,0,3:T(8,128)(2,1)S(1)} fusion(bf16[32,1,128,2,384]{2,4,3,0,1:T(8,128)(2,1)} %bitcast.89, bf16[32,1,128,2,384]{2,4,3,0,1:T(8,128)(2,1)} %bitcast.88), kind=kLoop, calls=%fused_computation.10 | loop fusion | flops 6291456 | bytes 25165824 | tf_op jit(solution)/shard_map/transpose | solution.py:71
  369.9 5.7 %copy.60 = bf16[32,128,2,2,384]{1,4,3,2,0:T(8,128)(2,1)} copy(bf16[32,128,2,2,384]{1,4,2,0,3:T(8,128)(2,1)S(1)} %maximum_bitcast_fusion) | data formatting | bytes 25165824 | tf_op jit(solution)/shard_map/transpose | solution.py:71
  375.7 16.6 %copy.61 = bf16[32,128,1536]{2,1,0:T(8,128)(2,1)} copy(bf16[32,128,1536]{1,2,0:T(8,128)(2,1)} %bitcast.85) | data formatting | bytes 25165824 | tf_op jit(solution)/shard_map/reshape | solution.py:71
  392.3 3.7 broadcast_in_dim.18
  396.0 36.8 %scatter_fusion.1 = bf16[19,128,1536]{2,1,0:T(8,128)(2,1)} fusion(bf16[19,128,1536]{2,1,0:T(8,128)(2,1)} %broadcast_in_dim.18, s32[32]{0:T(128)S(1)} %fusion.42, bf16[32,128,1536]{2,1,0:T(8,128)(2,1)} %copy.61), kind=kCustom, calls=%fused_computation.2 | custom fusion | bytes 37748864 | tf_op jit(solution)/shard_map/scatter | solution.py:76
  432.8 6.6 %slice_bitcast_fusion = bf16[18,1,128,1536]{3,2,1,0:T(8,128)(2,1)} fusion(bf16[19,128,1536]{2,1,0:T(8,128)(2,1)} %scatter_fusion.1), kind=kLoop, calls=%fused_computation.12 | loop fusion | bytes 14155776
  (95 shorter events, 39.8 us)
Async XLA Ops:
  7.2 180.6 %copy-start = (bf16[384,3072]{1,0:T(8,128)(2,1)S(1)}, bf16[384,3072]{1,0:T(8,128)(2,1)}, u32[]{:S(2)}) copy-start(bf16[384,3072]{1,0:T(8,128)(2,1)} %param.16) | copy-start | bytes 7077892
  7.2 52.1 %copy-start.2 = (bf16[512,384]{1,0:T(8,128)(2,1)S(1)}, bf16[512,384]{1,0:T(8,128)(2,1)}, u32[]{:S(2)}) copy-start(bf16[512,384]{1,0:T(8,128)(2,1)} %param.11) | copy-start | bytes 1179652
  7.2 25.3 %copy-start.15 = (s32[1,4]{1,0:T(1,128)S(1)}, s32[1,4]{1,0:T(1,128)}, u32[]{:S(2)}) copy-start(s32[1,4]{1,0:T(1,128)} %param.20) | copy-start | bytes 52
  7.2 35.4 %copy-start.11 = (s32[1,4]{1,0:T(1,128)S(1)}, s32[1,4]{1,0:T(1,128)}, u32[]{:S(2)}) copy-start(s32[1,4]{1,0:T(1,128)} %param.19) | copy-start | bytes 52
  7.2 27.8 %copy-start.10 = (s32[1,36]{1,0:T(1,128)S(1)}, s32[1,36]{1,0:T(1,128)}, u32[]{:S(2)}) copy-start(s32[1,36]{1,0:T(1,128)} %param.21) | copy-start | bytes 436
  24.6 18.1 %collective-permute-start.4 = (bf16[512,384]{1,0:T(8,128)(2,1)}, bf16[512,384]{1,0:T(8,128)(2,1)S(1)}, u32[]{:S(2)}, u32[]{:S(2)}) collective-permute-start(bf16[512,384]{1,0:T(8,128)(2,1)} %fusion.27), channel_id=1, source_target_pairs={{0,7},{1,0},{2,1},{3,2},{4,3},{5,4},{6,5},{7,6},{8,15},{9,8},{10,9... | collective-permute-start | bytes 1179656 | tf_op jit(solution)/shard_map/ppermute | solution.py:107
  27.5 5.0 %collective-permute-start = (bf16[512,384]{1,0:T(8,128)(2,1)}, bf16[512,384]{1,0:T(8,128)(2,1)}, u32[]{:S(2)}, u32[]{:S(2)}) collective-permute-start(bf16[512,384]{1,0:T(8,128)(2,1)} %fusion.27), channel_id=1, source_target_pairs={{0,1},{1,2},{2,3},{3,4},{4,5},{5,6},{6,7},{7,0},{8,9},{9,10},{10,1... | collective-permute-start | bytes 1179656 | tf_op jit(solution)/shard_map/ppermute | solution.py:105
  32.6 7.5 %collective-permute-start.1 = (bf16[512,384]{1,0:T(8,128)(2,1)}, bf16[512,384]{1,0:T(8,128)(2,1)S(1)}, u32[]{:S(2)}, u32[]{:S(2)}) collective-permute-start(bf16[512,384]{1,0:T(8,128)(2,1)} %collective-permute-done), channel_id=1, source_target_pairs={{0,1},{1,2},{2,3},{3,4},{4,5},{5,6},{6,7},{7,0},{8,9},{9,10},{10,1... | collective-permute-start | bytes 1179656 | tf_op jit(solution)/shard_map/ppermute | solution.py:105
  40.1 2.7 copy-start.5
  40.1 7.1 %collective-permute-start.2 = (bf16[512,384]{1,0:T(8,128)(2,1)S(1)}, bf16[512,384]{1,0:T(8,128)(2,1)}, u32[]{:S(2)}, u32[]{:S(2)}) collective-permute-start(bf16[512,384]{1,0:T(8,128)(2,1)S(1)} %collective-permute-done.1), channel_id=1, source_target_pairs={{0,1},{1,2},{2,3},{3,4},{4,5},{5,6},{6,7},{7,0},{8,9},{9,10},{10,1... | collective-permute-start | bytes 1179656 | tf_op jit(solution)/shard_map/ppermute | solution.py:105
  42.8 7.6 %collective-permute-start.5 = (bf16[512,384]{1,0:T(8,128)(2,1)S(1)}, bf16[512,384]{1,0:T(8,128)(2,1)}, u32[]{:S(2)}, u32[]{:S(2)}) collective-permute-start(bf16[512,384]{1,0:T(8,128)(2,1)S(1)} %collective-permute-done.4), channel_id=1, source_target_pairs={{0,7},{1,0},{2,1},{3,2},{4,3},{5,4},{6,5},{7,6},{8,15},{9,8},{10,9... | collective-permute-start | bytes 1179656 | tf_op jit(solution)/shard_map/ppermute | solution.py:107
  47.2 7.8 %collective-permute-start.3 = (bf16[512,384]{1,0:T(8,128)(2,1)}, bf16[512,384]{1,0:T(8,128)(2,1)}, u32[]{:S(2)}, u32[]{:S(2)}) collective-permute-start(bf16[512,384]{1,0:T(8,128)(2,1)} %collective-permute-done.2), channel_id=1, source_target_pairs={{0,1},{1,2},{2,3},{3,4},{4,5},{5,6},{6,7},{7,0},{8,9},{9,10},{10,1... | collective-permute-start | bytes 1179656 | tf_op jit(solution)/shard_map/ppermute | solution.py:105
  49.8 13.2 %copy-start.6 = (bf16[512,384]{1,0:T(8,128)(2,1)S(1)}, bf16[512,384]{1,0:T(8,128)(2,1)}, u32[]{:S(2)}) copy-start(bf16[512,384]{1,0:T(8,128)(2,1)} %copy-done.5) | copy-start | bytes 1179652
  50.3 15.6 %copy-start.12 = (bf16[3072,384]{1,0:T(8,128)(2,1)S(1)}, bf16[3072,384]{1,0:T(8,128)(2,1)}, u32[]{:S(2)}) copy-start(bf16[3072,384]{1,0:T(8,128)(2,1)} %param.15) | copy-start | bytes 7077892
  50.4 10.3 %collective-permute-start.6 = (bf16[512,384]{1,0:T(8,128)(2,1)}, bf16[512,384]{1,0:T(8,128)(2,1)S(1)}, u32[]{:S(2)}, u32[]{:S(2)}) collective-permute-start(bf16[512,384]{1,0:T(8,128)(2,1)} %collective-permute-done.5), channel_id=1, source_target_pairs={{0,7},{1,0},{2,1},{3,2},{4,3},{5,4},{6,5},{7,6},{8,15},{9,8},{10,9... | collective-permute-start | bytes 1179656 | tf_op jit(solution)/shard_map/ppermute | solution.py:107
  63.1 5.4 %copy-start.13 = (bf16[3072,384]{1,0:T(8,128)(2,1)S(1)}, bf16[3072,384]{1,0:T(8,128)(2,1)}, u32[]{:S(2)}) copy-start(bf16[3072,384]{1,0:T(8,128)(2,1)} %param.13) | copy-start | bytes 7077892
  68.4 2.0 copy-start.14
  74.3 9.9 %copy-start.7 = (bf16[512,384]{1,0:T(8,128)(2,1)S(1)}, bf16[512,384]{1,0:T(8,128)(2,1)}, u32[]{:S(2)}) copy-start(bf16[512,384]{1,0:T(8,128)(2,1)} %fusion.15) | copy-start | bytes 1179652
  86.5 7.1 %copy-start.1 = (bf16[4608,384]{1,0:T(8,128)(2,1)}, bf16[4608,384]{1,0:T(8,128)(2,1)S(1)}, u32[]{:S(2)}) copy-start(bf16[4608,384]{1,0:T(8,128)(2,1)S(1)} %pad_maximum_fusion.1) | copy-start | bytes 10616836
  122.1 7.8 %copy-start.8 = (bf16[512,4,48]{0,2,1:T(8,128)(2,1)S(1)}, bf16[512,4,48]{0,2,1:T(8,128)(2,1)}, u32[]{:S(2)}) copy-start(bf16[512,4,48]{0,2,1:T(8,128)(2,1)} %get-tuple-element.16) | copy-start | bytes 589828
  122.1 7.8 %copy-start.9 = (bf16[512,4,48]{0,2,1:T(8,128)(2,1)S(1)}, bf16[512,4,48]{0,2,1:T(8,128)(2,1)}, u32[]{:S(2)}) copy-start(bf16[512,4,48]{0,2,1:T(8,128)(2,1)} %get-tuple-element.17) | copy-start | bytes 589828
  122.1 178.4 %all-to-all-start.1 = ((bf16[64,128,768]{2,1,0:T(8,128)(2,1)}), bf16[64,128,768]{2,1,0:T(8,128)(2,1)}, u32[]{:S(2)}, u32[]{:S(2)}) async-start(bf16[64,128,768]{2,1,0:T(8,128)(2,1)} %scatter_fusion), calls=%async_computation.2 | async-start | bytes 25165824 | tf_op jit(solution)/shard_map/all_to_all | solution.py:179
  129.8 204.3 %reduce-scatter.2.cloned.1.call-start = ((), (), s32[]{:S(2)}) async-start(), calls=%async_computation.3 | async-start | bytes 7077888 | tf_op jit(solution)/shard_map/reduce_scatter | solution.py:147
  154.2 18.2 %copy-start.3 = (pred[512,4608]{1,0:T(8,128)(4,1)S(1)}, pred[512,4608]{1,0:T(8,128)(4,1)}, u32[]{:S(2)}) copy-start(pred[512,4608]{1,0:T(8,128)(4,1)} %pad_add_fusion) | copy-start | bytes 7077892
  154.2 18.2 %copy-start.4 = (bf16[4608,384]{0,1:T(8,128)(2,1)S(1)}, bf16[4608,384]{0,1:T(8,128)(2,1)}, u32[]{:S(2)}) copy-start(bf16[4608,384]{0,1:T(8,128)(2,1)} %copy.52) | copy-start | bytes 10616836
  311.1 25.0 %collective-permute-start.7 = (bf16[32,128,768]{2,1,0:T(8,128)(2,1)}, bf16[32,128,768]{2,1,0:T(8,128)(2,1)}, u32[]{:S(2)}, u32[]{:S(2)}) collective-permute-start(bf16[32,128,768]{2,1,0:T(8,128)(2,1)} %bitcast.90), channel_id=1, source_target_pairs={{0,1},{1,0},{2,3},{3,2},{4,5},{5,4},{6,7},{7,6},{8,9},{9,8},{10,11... | collective-permute-start | bytes 18874376 | tf_op jit(solution)/shard_map/ppermute | solution.py:17
  321.0 12.8 %all-to-all-start = ((s32[16,4,1]{1,2,0:T(1,128)}), s32[16,4,1]{1,2,0:T(1,128)S(1)}, u32[]{:S(2)}, u32[]{:S(2)}) async-start(s32[16,4,1]{1,2,0:T(1,128)} %bitcast.23), calls=%async_computation.1 | async-start | bytes 16384 | tf_op jit(solution)/shard_map/all_to_all | solution.py:180
Sparse Core Ops, SparseCore 0:
  192.5 47.8 reduce-scatter.1
